TPU v7x, 128 devices: a whole 4x4x4 slice. The times are simulated.
128 devices in a mesh: dp: 2 (over core), seq: 16 (over z, x), head: 4 (over y).
Axes of the slice: x: 4, y: 4, z: 4, core: 2. Of those that a mesh axis runs over, the one named last changes fastest.
Arguments:
- queries: bfloat16 [2, 10240, 2048], P('dp', ('seq', 'head')), may hold values from -45 to 45
- key_rows: bfloat16 [2, 10240, 2048], P('dp', ('seq', 'head')), may hold values from -6 to 6
- values: bfloat16 [2, 10240, 2048], P('dp', ('seq', 'head')), may hold values from -6 to 6
- rand_blocks: int32 [160, 16, 4], P('seq', 'head'), may hold values from 0 to 159, as said below
- out_weight: bfloat16 [2048, 2048], P('head'), may hold values from -0.125 to 0.125
- cotangent: bfloat16 [2, 10240, 2048], P('dp', ('seq', 'head')), may hold values from -6 to 6
Outputs:
- layer_out: bfloat16 [2, 10240, 2048], P('dp', ('seq', 'head'))
- grad_queries: bfloat16 [2, 10240, 2048], P('dp', ('seq', 'head'))
- grad_keys: bfloat16 [2, 10240, 2048], P('dp', ('seq', 'head'))
- grad_values: bfloat16 [2, 10240, 2048], P('dp', ('seq', 'head'))
- weight_grad: float32 [2048, 2048], P('head')
Inputs may be any that keep to these rules, and one draw needn't show every extreme that they name: `rand_blocks`: key block b lies in range b // 10 of seq. Over the 10 query blocks of one index of seq and the 4 heads of one index of head, at most 15 of the listed random blocks lie in any one range of seq; in every draw, for every index of head, some range of seq receives exactly 15 of them from every index of seq.
All inputs are finite; a program needn't handle non-finite values.
Results may differ from a plain program's by a relative error of at most 0.034.
Values may be sent and summed in bfloat16 or wider, within the bound.
No kernel may reach another device: no remote copies, remote signals or barrier semaphores. Data moves between devices by JAX's collectives and lax.ppermute only.
A program may use at most 192 MiB of HBM per device.

v0:
```python
import math
import jax
import jax.numpy as jnp
from jax import lax
from jax.sharding import PartitionSpec as P

HEAD_SIZE = 128
BLOCK_TOKENS = 64


def with_halo(block, sides, width):
    for axis, dim in sides:
        count = lax.axis_size(axis)
        forward = [(i, i + 1) for i in range(count - 1)]
        backward = [(target, source) for source, target in forward]
        low = lax.ppermute(
            lax.slice_in_dim(block, block.shape[dim] - width, None, axis=dim), axis, forward
        )
        high = lax.ppermute(lax.slice_in_dim(block, 0, width, axis=dim), axis, backward)
        block = jnp.concatenate([low, block, high], axis=dim)
    return block


def broadcast_first(block, axis):
    count = lax.axis_size(axis)
    index = lax.axis_index(axis)
    step = 1
    while step < count:
        pairs = [(i, i + step) for i in range(step) if i + step < count]
        got = lax.ppermute(block, axis, pairs)
        block = jnp.where(index >= step, got, block)
        step *= 2
    return block


def reduce_to_first(block, axis):
    count = lax.axis_size(axis)
    step = 1
    while step * 2 < count:
        step *= 2
    while step >= 1:
        pairs = [(i + step, i) for i in range(step) if i + step < count]
        block = block + lax.ppermute(block, axis, pairs)
        step //= 2
    return block


def per_device(queries, key_rows, values, rand_blocks, out_weight, cotangent):
    block_len = BLOCK_TOKENS
    head_dim = HEAD_SIZE
    seq_count = lax.axis_size("seq")
    seq_index = lax.axis_index("seq")
    q_heads, k_heads, v_heads = (
        lax.all_to_all(queries, "head", split_axis=2, concat_axis=1, tiled=True),
        lax.all_to_all(key_rows, "head", split_axis=2, concat_axis=1, tiled=True),
        lax.all_to_all(values, "head", split_axis=2, concat_axis=1, tiled=True),
    )
    q_rows = q_heads[0]
    shard_len = q_rows.shape[0]
    width_cols = q_rows.shape[1]
    head_count = width_cols // head_dim
    block_count = shard_len // block_len
    rand_count = rand_blocks.shape[2]
    key_value = jnp.concatenate([k_heads[0], v_heads[0]], axis=1)
    padded = with_halo(key_value, (("seq", 0),), block_len)
    first_block = broadcast_first(key_value[:block_len], "seq")
    requests = jnp.transpose(rand_blocks, (0, 2, 1)).reshape(-1)
    request_count = requests.shape[0]
    head_of = jnp.arange(request_count, dtype=jnp.int32) % head_count
    capacity = 3 * request_count // (2 * seq_count)
    owners = requests // block_count
    offsets = requests % block_count
    one_hot = (owners[:, None] == jnp.arange(seq_count, dtype=jnp.int32)[None, :]).astype(jnp.int32)
    position = jnp.sum(one_hot * (jnp.cumsum(one_hot, axis=0) - 1), axis=1)
    slot_of = owners * capacity + position
    asked_codes = (
        jnp.full((seq_count * capacity,), -1, jnp.int32)
        .at[slot_of]
        .set(offsets * head_count + head_of)
        .reshape(seq_count, capacity)
    )
    asked_here = lax.all_to_all(asked_codes, "seq", split_axis=0, concat_axis=0, tiled=True)
    slot_total = seq_count * capacity
    pair_count = block_count * head_count
    asked_flat = asked_here.reshape(slot_total)
    serve_hot = (asked_flat[:, None] == jnp.arange(pair_count, dtype=jnp.int32)[None, :]).astype(
        jnp.bfloat16
    )
    pick_hot = (slot_of[:, None] == jnp.arange(slot_total, dtype=jnp.int32)[None, :]).astype(
        jnp.bfloat16
    )
    kv_pairs = jnp.transpose(
        key_value.reshape(block_count, block_len, 2, head_count, head_dim), (0, 3, 1, 2, 4)
    ).reshape(pair_count, block_len * 2 * head_dim)
    served = jnp.dot(serve_hot, kv_pairs, preferred_element_type=jnp.float32).astype(jnp.bfloat16)
    served = served.reshape(seq_count, capacity, block_len, 2 * head_dim)
    received = lax.all_to_all(served, "seq", split_axis=0, concat_axis=0, tiled=True)
    far_pairs = jnp.dot(
        pick_hot, received.reshape(slot_total, -1), preferred_element_type=jnp.float32
    ).astype(jnp.bfloat16)
    pair_view = padded.reshape(block_count + 2, block_len, 2, head_count, head_dim)
    window_pairs = jnp.stack(
        [pair_view[:block_count], pair_view[1 : block_count + 1], pair_view[2:]], axis=1
    ).reshape(block_count, 3 * block_len, 2, head_count, head_dim)
    window_keys = window_pairs[:, :, 0]
    window_vals = window_pairs[:, :, 1]
    first_pairs = first_block.reshape(block_len, 2, head_count, head_dim)
    first_keys = first_pairs[:, 0]
    first_vals = first_pairs[:, 1]
    far_view = far_pairs.reshape(block_count, rand_count, head_count, block_len, 2 * head_dim)
    far_keys = far_view[..., :head_dim]
    far_vals = far_view[..., head_dim:]
    global_ids = seq_index * block_count + jnp.arange(block_count, dtype=jnp.int32)
    block_total = seq_count * block_count
    window_live = jnp.stack([global_ids > 0, global_ids >= 0, global_ids < block_total - 1], axis=1)
    window_mask = jnp.repeat(window_live, block_len, axis=1)[None, :, None, :]
    query_blocks = q_rows.reshape(block_count, block_len, head_count, head_dim)
    softmax_scale = 1.0 / math.sqrt(head_dim)
    score_window = (
        jnp.einsum("ibhd,ikhd->hibk", query_blocks, window_keys, preferred_element_type=jnp.float32)
        * softmax_scale
    )
    score_first = (
        jnp.einsum("ibhd,khd->hibk", query_blocks, first_keys, preferred_element_type=jnp.float32)
        * softmax_scale
    )
    score_far = (
        jnp.einsum("ibhd,irhtd->hibrt", query_blocks, far_keys, preferred_element_type=jnp.float32)
        * softmax_scale
    )
    max_window = jnp.max(jnp.where(window_mask, score_window, -jnp.inf), axis=-1, keepdims=True)
    max_first = jnp.max(score_first, axis=-1, keepdims=True)
    max_far = jnp.max(score_far, axis=(-2, -1))[..., None]
    row_max = jnp.maximum(jnp.maximum(max_window, max_first), max_far)
    weight_window = jnp.where(window_mask, jnp.exp(score_window - row_max), 0.0)
    weight_first = jnp.exp(score_first - row_max)
    weight_far = jnp.exp(score_far - row_max[..., None])
    totals = (
        jnp.sum(weight_window, axis=-1, keepdims=True)
        + jnp.sum(weight_first, axis=-1, keepdims=True)
        + jnp.sum(weight_far, axis=(-2, -1))[..., None]
    )
    mixed = jnp.einsum(
        "hibk,ikhd->ibhd",
        weight_window.astype(jnp.bfloat16),
        window_vals,
        preferred_element_type=jnp.float32,
    )
    mixed = mixed + jnp.einsum(
        "hibk,khd->ibhd",
        weight_first.astype(jnp.bfloat16),
        first_vals,
        preferred_element_type=jnp.float32,
    )
    mixed = mixed + jnp.einsum(
        "hibrt,irhtd->ibhd",
        weight_far.astype(jnp.bfloat16),
        far_vals,
        preferred_element_type=jnp.float32,
    )
    totals_rows = jnp.transpose(totals, (1, 2, 0, 3))
    attn = (mixed / totals_rows).astype(jnp.bfloat16)
    logsum = row_max + jnp.log(totals)
    attn_rows = attn.reshape(shard_len, width_cols)
    layer_out = lax.psum_scatter(
        jnp.dot(attn_rows, out_weight, preferred_element_type=jnp.float32),
        "head",
        scatter_dimension=0,
        tiled=True,
    ).astype(jnp.bfloat16)[None]
    piece_flat = lax.all_gather(cotangent, "head", axis=1, tiled=True)[0]
    grad_piece = jnp.dot(piece_flat, out_weight.T, preferred_element_type=jnp.float32).astype(
        jnp.bfloat16
    )
    weight_acc = jnp.dot(attn_rows.T, piece_flat, preferred_element_type=jnp.float32)
    token_total = lax.axis_size("dp") * seq_count * shard_len
    weight_grad = lax.psum(weight_acc, ("dp", "seq")) * (1.0 / math.sqrt(token_total))
    grad_blocks = grad_piece.reshape(block_count, block_len, head_count, head_dim)
    delta_rows = jnp.sum(grad_blocks.astype(jnp.float32) * attn.astype(jnp.float32), axis=-1)
    row_delta = jnp.transpose(delta_rows, (2, 0, 1))[..., None]
    prob_window = jnp.where(window_mask, jnp.exp(score_window - logsum), 0.0)
    prob_first = jnp.exp(score_first - logsum)
    prob_far = jnp.exp(score_far - logsum[..., None])
    dprob_window = jnp.einsum(
        "ibhd,ikhd->hibk", grad_blocks, window_vals, preferred_element_type=jnp.float32
    )
    dprob_first = jnp.einsum(
        "ibhd,khd->hibk", grad_blocks, first_vals, preferred_element_type=jnp.float32
    )
    dprob_far = jnp.einsum(
        "ibhd,irhtd->hibrt", grad_blocks, far_vals, preferred_element_type=jnp.float32
    )
    dscore_window = (prob_window * (dprob_window - row_delta)).astype(jnp.bfloat16)
    dscore_first = (prob_first * (dprob_first - row_delta)).astype(jnp.bfloat16)
    dscore_far = (prob_far * (dprob_far - row_delta[..., None])).astype(jnp.bfloat16)
    grad_q = jnp.einsum(
        "hibk,ikhd->ibhd", dscore_window, window_keys, preferred_element_type=jnp.float32
    )
    grad_q = grad_q + jnp.einsum(
        "hibk,khd->ibhd", dscore_first, first_keys, preferred_element_type=jnp.float32
    )
    grad_q = grad_q + jnp.einsum(
        "hibrt,irhtd->ibhd", dscore_far, far_keys, preferred_element_type=jnp.float32
    )
    grad_q = (grad_q * softmax_scale).astype(jnp.bfloat16)
    key_window = (
        jnp.einsum(
            "hibk,ibhd->ikhd", dscore_window, query_blocks, preferred_element_type=jnp.float32
        )
        * softmax_scale
    )
    value_window = jnp.einsum(
        "hibk,ibhd->ikhd",
        prob_window.astype(jnp.bfloat16),
        grad_blocks,
        preferred_element_type=jnp.float32,
    )
    key_first = (
        jnp.einsum("hibk,ibhd->khd", dscore_first, query_blocks, preferred_element_type=jnp.float32)
        * softmax_scale
    )
    value_first = jnp.einsum(
        "hibk,ibhd->khd",
        prob_first.astype(jnp.bfloat16),
        grad_blocks,
        preferred_element_type=jnp.float32,
    )
    key_far = (
        jnp.einsum(
            "hibrt,ibhd->irhtd", dscore_far, query_blocks, preferred_element_type=jnp.float32
        )
        * softmax_scale
    )
    value_far = jnp.einsum(
        "hibrt,ibhd->irhtd",
        prob_far.astype(jnp.bfloat16),
        grad_blocks,
        preferred_element_type=jnp.float32,
    )
    window_terms = jnp.stack(
        [
            key_window.reshape(block_count, 3, block_len, head_count, head_dim),
            value_window.reshape(block_count, 3, block_len, head_count, head_dim),
        ],
        axis=3,
    )
    grad_pad = jnp.zeros((block_count + 2, block_len, 2, head_count, head_dim), jnp.float32)
    grad_pad = (
        grad_pad.at[:block_count]
        .add(window_terms[:, 0])
        .at[1 : block_count + 1]
        .add(window_terms[:, 1])
        .at[2:]
        .add(window_terms[:, 2])
    )
    global_grad = reduce_to_first(
        jnp.stack([key_first, value_first], axis=1).reshape(block_len, 2 * width_cols), "seq"
    ).reshape(block_len, 2, head_count, head_dim)
    grad_pad = grad_pad.at[1].add(jnp.where(seq_index == 0, global_grad, 0.0))
    rims = jnp.concatenate([grad_pad[0], grad_pad[block_count + 1]], axis=0).reshape(
        2 * block_len, 2 * width_cols
    )
    rim_sums = with_halo(rims.astype(jnp.bfloat16), (("seq", 0),), block_len).astype(rims.dtype)
    core = grad_pad[1 : block_count + 1].reshape(shard_len, 2 * width_cols)
    core = (
        core.at[:block_len]
        .add(rim_sums[:block_len])
        .at[shard_len - block_len :]
        .add(rim_sums[3 * block_len :])
    )
    core = core.reshape(block_count, block_len, 2, head_count, head_dim)
    far_terms = (
        jnp.concatenate([key_far, value_far], axis=-1)
        .reshape(request_count, block_len * 2 * head_dim)
        .astype(jnp.bfloat16)
    )
    outgoing = jnp.dot(pick_hot.T, far_terms, preferred_element_type=jnp.float32).astype(
        jnp.bfloat16
    )
    outgoing = outgoing.reshape(seq_count, capacity, block_len, 2 * head_dim)
    incoming = lax.all_to_all(outgoing, "seq", split_axis=0, concat_axis=0, tiled=True)
    added = jnp.dot(
        serve_hot.T, incoming.reshape(slot_total, -1), preferred_element_type=jnp.float32
    ).reshape(block_count, head_count, block_len, 2, head_dim)
    core = core + jnp.transpose(added, (0, 2, 3, 1, 4))
    grad_k = core[:, :, 0].reshape(shard_len, width_cols).astype(jnp.bfloat16)
    grad_v = core[:, :, 1].reshape(shard_len, width_cols).astype(jnp.bfloat16)
    grad_q_rows = grad_q.reshape(shard_len, width_cols)
    grad_queries, grad_keys, grad_values = (
        lax.all_to_all(grad_q_rows[None], "head", split_axis=1, concat_axis=2, tiled=True),
        lax.all_to_all(grad_k[None], "head", split_axis=1, concat_axis=2, tiled=True),
        lax.all_to_all(grad_v[None], "head", split_axis=1, concat_axis=2, tiled=True),
    )
    return (layer_out, grad_queries, grad_keys, grad_values, weight_grad)


def solution(mesh):
    in_specs = (
        P("dp", ("seq", "head"), None),
        P("dp", ("seq", "head"), None),
        P("dp", ("seq", "head"), None),
        P("seq", "head", None),
        P("head", None),
        P("dp", ("seq", "head"), None),
    )
    out_specs = (
        P("dp", ("seq", "head"), None),
        P("dp", ("seq", "head"), None),
        P("dp", ("seq", "head"), None),
        P("dp", ("seq", "head"), None),
        P("head", None),
    )
    return jax.shard_map(
        per_device, mesh=mesh, in_specs=in_specs, out_specs=out_specs, check_vma=False
    )
```

profile of v0, /device:TPU:0, one launch (start us, length us, event | category | flops | bytes accessed | tf_op | source)
XLA Modules:
  0.0 644.7 jit_solution(16865927430126323125)
XLA Ops:
  7.2 6.0 copy.227
  13.7 12.7 %reduce.20 = bf16[2048,160]{1,0:T(8,128)(2,1)S(1)} reduce(bf16[2048,1,160]{2,1,0:T(2,128)(2,1)} %bitcast.285, bf16[]{:T(256)} %broadcast.366), dimensions={1}, to_apply=%bitcast.240.reduce_sub_computation | reduce | bytes 1310722
  34.1 5.9 copy.230
  39.9 12.6 %reduce.21 = bf16[2048,160]{1,0:T(8,128)(2,1)S(1)} reduce(bf16[2048,1,160]{2,1,0:T(2,128)(2,1)} %bitcast.289, bf16[]{:T(256)} %broadcast.366), dimensions={1}, to_apply=%bitcast.238.reduce_sub_computation | reduce | bytes 1310722
  55.0 4.8 all-to-all-start.1
  74.8 5.7 copy.231
  90.1 9.4 %all-to-all-start.3 = ((s32[16,1,15]{2,1,0:T(1,128)}), s32[16,1,15]{2,1,0:T(1,128)S(1)}, u32[]{:S(2)}, u32[]{:S(2)}) async-start(s32[16,1,15]{2,1,0:T(1,128)} %bitcast.19), calls=%async_computation.3 | async-start | bytes 16384 | tf_op jit(solution)/shard_map/all_to_all | solution.py:82
  99.5 5.9 copy.235
  105.4 12.6 %reduce.19 = bf16[2048,160]{1,0:T(8,128)(2,1)S(1)} reduce(bf16[2048,1,160]{2,1,0:T(2,128)(2,1)} %bitcast.290, bf16[]{:T(256)} %broadcast.366), dimensions={1}, to_apply=%bitcast.242.reduce_sub_computation | reduce | bytes 1310722
  120.4 4.8 all-to-all-start.2
  141.6 6.7 %convolution_convert_fusion.1 = bf16[240,16384]{1,0:T(8,128)(2,1)} fusion(bf16[40,16384]{1,0:T(8,128)(2,1)} %reshape.545, s32[240]{0:T(256)S(1)} %eq.85), kind=kOutput, calls=%fused_computation.2 | convolution fusion | flops 318514560 | bytes 9176000 | tf_op jit(solution)/shard_map/dot_general | solution.py:95
  148.2 8.7 %copy.340 = bf16[30,8,64,256]{3,2,1,0:T(8,128)(2,1)} copy(bf16[30,8,64,256]{3,1,2,0:T(8,128)(2,1)} %bitcast.266) | data formatting | bytes 15728640
  156.9 7.3 %all-to-all-start.4 = ((bf16[16,15,64,256]{3,2,1,0:T(8,128)(2,1)}), bf16[16,15,64,256]{3,2,1,0:T(8,128)(2,1)}, u32[]{:S(2)}, u32[]{:S(2)}) async-start(bf16[16,15,64,256]{3,2,1,0:T(8,128)(2,1)} %bitcast.269), calls=%async_computation.4 | async-start | bytes 15728640 | tf_op jit(solution)/shard_map/all_to_all | solution.py:97
  175.1 5.7 copy.236
  189.7 78.3 %collective-permute-done.2 = bf16[64,1024]{1,0:T(8,128)(2,1)} collective-permute-done((bf16[64,1024]{1,0:T(8,128)(2,1)S(1)}, bf16[64,1024]{1,0:T(8,128)(2,1)}, u32[]{:S(2)}, u32[]{:S(2)}) %collective-permute-start.2) | collective-permute-done | bytes 131104 | tf_op jit(solution)/shard_map/ppermute | solution.py:30
  275.6 4.9 pad_maximum_fusion.1
  299.3 14.4 %copy.341 = bf16[30,8,64,256]{3,1,2,0:T(8,128)(2,1)} copy(bf16[30,8,64,256]{3,2,1,0:T(8,128)(2,1)} %bitcast.108) | data formatting | bytes 15728640
  342.7 5.0 multiply_convert_fusion.1
  366.6 5.6 convolution_convert_fusion
  372.2 8.9 %copy.345 = bf16[30,8,64,256]{3,2,1,0:T(8,128)(2,1)} copy(bf16[30,8,64,256]{3,1,2,0:T(8,128)(2,1)} %bitcast.265) | data formatting | bytes 15728640
  381.1 9.6 %all-to-all-start.6 = ((bf16[16,15,64,256]{3,2,1,0:T(8,128)(2,1)}), bf16[16,15,64,256]{3,2,1,0:T(8,128)(2,1)}, u32[]{:S(2)}, u32[]{:S(2)}) async-start(bf16[16,15,64,256]{3,2,1,0:T(8,128)(2,1)} %bitcast.268), calls=%async_computation.7 | async-start | bytes 15728640 | tf_op jit(solution)/shard_map/all_to_all | solution.py:281
  411.1 60.6 %collective-permute-done.6 = f32[64,1024]{1,0:T(8,128)S(1)} collective-permute-done((f32[64,1024]{1,0:T(8,128)}, f32[64,1024]{1,0:T(8,128)S(1)}, u32[]{:S(2)}, u32[]{:S(2)}) %collective-permute-start.6) | collective-permute-done | bytes 262176 | tf_op jit(solution)/shard_map/ppermute | solution.py:43
  475.6 13.3 %collective-permute-done.7 = f32[64,1024]{1,0:T(8,128)S(1)} collective-permute-done((f32[64,1024]{1,0:T(8,128)S(1)}, f32[64,1024]{1,0:T(8,128)S(1)}, u32[]{:S(2)}, u32[]{:S(2)}) %collective-permute-start.7) | collective-permute-done | bytes 262176 | tf_op jit(solution)/shard_map/ppermute | solution.py:43
  492.4 13.0 %collective-permute-done.8 = f32[64,1024]{1,0:T(8,128)S(1)} collective-permute-done((f32[64,1024]{1,0:T(8,128)S(1)}, f32[64,1024]{1,0:T(8,128)S(1)}, u32[]{:S(2)}, u32[]{:S(2)}) %collective-permute-start.8) | collective-permute-done | bytes 262176 | tf_op jit(solution)/shard_map/ppermute | solution.py:43
  508.1 8.7 %collective-permute-done.9 = f32[64,1024]{1,0:T(8,128)S(1)} collective-permute-done((f32[64,1024]{1,0:T(8,128)S(1)}, f32[64,1024]{1,0:T(8,128)S(1)}, u32[]{:S(2)}, u32[]{:S(2)}) %collective-permute-start.9) | collective-permute-done | bytes 262176 | tf_op jit(solution)/shard_map/ppermute | solution.py:43
  524.6 5.2 collective-permute-start.10
  559.2 14.5 %copy.346 = bf16[30,8,64,256]{3,1,2,0:T(8,128)(2,1)} copy(bf16[30,8,64,256]{3,2,1,0:T(8,128)(2,1)} %bitcast.123) | data formatting | bytes 15728640
  573.7 13.9 %dot_general.103 = bf16[64,2,128,240]{2,1,0,3:T(2,128)(2,1)} reshape(bf16[16384,240]{0,1:T(8,128)(2,1)} %bitcast.270) | data formatting | bytes 15728640 | tf_op jit(solution)/shard_map/dot_general | solution.py:282
  587.6 10.2 %fusion.8 = bf16[10,64,2,4,128]{4,0,2,1,3:T(8,128)(2,1)S(1)} fusion(f32[10,64,2,4,128]{4,3,2,1,0:T(4,128)} %reshape.556, bf16[64,2,128,240]{2,1,0,3:T(2,128)(2,1)} %dot_general.103, s32[10,4]{0,1:T(4,128)S(1)} %multiply_add_fusion, s32[240]{0:T(256)S(1)} %eq.85), kind=kOutput, calls=%fused_computation.19 | convolution fusion | flops 315893120 | bytes 11797600 | tf_op jit(solution)/shard_map/dot_general | solution.py:282
  605.0 4.9 all-to-all-start.8
  620.1 4.8 all-to-all-start.7
  624.9 5.0 broadcast_multiply_fusion
  (256 shorter events, 239.9 us)
Async XLA Ops:
  7.2 286.1 %copy-start = (bf16[512,2048]{1,0:T(8,128)(2,1)S(1)}, bf16[512,2048]{1,0:T(8,128)(2,1)}, u32[]{:S(2)}) copy-start(bf16[512,2048]{1,0:T(8,128)(2,1)} %param.22) | copy-start | bytes 6291460
  13.7 19.6 %copy-start.30 = (s32[10,4,4]{0,2,1:T(4,128)S(1)}, s32[10,4,4]{0,2,1:T(4,128)}, u32[]{:S(2)}) copy-start(s32[10,4,4]{0,2,1:T(4,128)} %param.21) | copy-start | bytes 1924
  28.7 26.2 %all-to-all-start = ((bf16[4,2,40960]{2,1,0:T(2,128)(2,1)}), bf16[4,2,40960]{2,1,0:T(2,128)(2,1)}, u32[]{:S(2)}, u32[]{:S(2)}) async-start(bf16[4,2,40960]{2,1,0:T(2,128)(2,1)} %reshape.595), calls=%async_computation | async-start | bytes 1310720 | tf_op jit(solution)/shard_map/all_to_all | solution.py:55
  55.0 15.4 %all-to-all-start.1 = ((bf16[4,2,40960]{2,1,0:T(2,128)(2,1)}), bf16[4,2,40960]{2,1,0:T(2,128)(2,1)}, u32[]{:S(2)}, u32[]{:S(2)}) async-start(bf16[4,2,40960]{2,1,0:T(2,128)(2,1)} %reshape.593), calls=%async_computation.1 | async-start | bytes 1310720 | tf_op jit(solution)/shard_map/all_to_all | solution.py:56
  61.1 27.2 %copy-start.32 = (s32[160]{0:T(256)}, s32[160]{0:T(256)S(1)}, u32[]{:S(2)}) copy-start(s32[160]{0:T(256)S(1)} %fusion.135) | copy-start | bytes 1924
  70.4 12.4 %copy-start.18 = (bf16[1,4,160,512]{3,2,1,0:T(8,128)(2,1)}, bf16[1,4,160,512]{3,2,1,0:T(8,128)(2,1)S(1)}, u32[]{:S(2)}) copy-start(bf16[1,4,160,512]{3,2,1,0:T(8,128)(2,1)S(1)} %copy.229) | copy-start | bytes 1966084
  83.6 42.9 %collective-permute-start = (bf16[64,1024]{1,0:T(8,128)(2,1)S(1)}, bf16[64,1024]{1,0:T(8,128)(2,1)S(1)}, u32[]{:S(2)}, u32[]{:S(2)}) collective-permute-start(bf16[64,1024]{1,0:T(8,128)(2,1)S(1)} %get-tuple-element.96), channel_id=1, source_target_pairs={{0,4},{4,8},{8,12},{12,16},{16,20},{20,24},{24,28},{28,32},{32,36}... | collective-permute-start | bytes 393224 | tf_op jit(solution)/shard_map/ppermute | solution.py:16
  87.0 40.1 %collective-permute-start.1 = (bf16[64,1024]{1,0:T(8,128)(2,1)S(1)}, bf16[64,1024]{1,0:T(8,128)(2,1)}, u32[]{:S(2)}, u32[]{:S(2)}) collective-permute-start(bf16[64,1024]{1,0:T(8,128)(2,1)S(1)} %get-tuple-element.97), channel_id=1, source_target_pairs={{4,0},{8,4},{12,8},{16,12},{20,16},{24,20},{28,24},{32,28},{36,32}... | collective-permute-start | bytes 393224 | tf_op jit(solution)/shard_map/ppermute | solution.py:19
  90.1 30.3 %all-to-all-start.3 = ((s32[16,1,15]{2,1,0:T(1,128)}), s32[16,1,15]{2,1,0:T(1,128)S(1)}, u32[]{:S(2)}, u32[]{:S(2)}) async-start(s32[16,1,15]{2,1,0:T(1,128)} %bitcast.19), calls=%async_computation.3 | async-start | bytes 16384 | tf_op jit(solution)/shard_map/all_to_all | solution.py:82
  120.4 36.6 %all-to-all-start.2 = ((bf16[4,2,40960]{2,1,0:T(2,128)(2,1)}), bf16[4,2,40960]{2,1,0:T(2,128)(2,1)}, u32[]{:S(2)}, u32[]{:S(2)}) async-start(bf16[4,2,40960]{2,1,0:T(2,128)(2,1)} %reshape.597), calls=%async_computation.2 | async-start | bytes 1310720 | tf_op jit(solution)/shard_map/all_to_all | solution.py:54
  156.9 142.3 %all-to-all-start.4 = ((bf16[16,15,64,256]{3,2,1,0:T(8,128)(2,1)}), bf16[16,15,64,256]{3,2,1,0:T(8,128)(2,1)}, u32[]{:S(2)}, u32[]{:S(2)}) async-start(bf16[16,15,64,256]{3,2,1,0:T(8,128)(2,1)} %bitcast.269), calls=%async_computation.4 | async-start | bytes 15728640 | tf_op jit(solution)/shard_map/all_to_all | solution.py:97
  164.2 129.1 %all-gather.2.cloned.1.call-start = ((), (), s32[]{:S(2)}) async-start(), calls=%async_computation.11 | async-start | bytes 3276800 | tf_op jit(solution)/shard_map/all_gather | solution.py:171
  164.9 460.0 %all-reduce.4.cloned.1.call-start = ((), (), s32[]{:S(2)}) async-start(), calls=%async_computation.12 | async-start | bytes 8388608 | tf_op jit(solution)/shard_map/psum | solution.py:177
  165.7 102.3 %collective-permute-start.2 = (bf16[64,1024]{1,0:T(8,128)(2,1)S(1)}, bf16[64,1024]{1,0:T(8,128)(2,1)}, u32[]{:S(2)}, u32[]{:S(2)}) collective-permute-start(bf16[64,1024]{1,0:T(8,128)(2,1)S(1)} %get-tuple-element.97), channel_id=1, source_target_pairs={{0,4},{1,5},{2,6},{3,7},{64,68},{65,69},{66,70},{67,71}} | collective-permute-start | bytes 393224 | tf_op jit(solution)/shard_map/ppermute | solution.py:30
  189.7 84.1 %copy-start.20 = (bf16[640,1024]{1,0:T(8,128)(2,1)S(1)}, bf16[640,1024]{1,0:T(8,128)(2,1)}, u32[]{:S(2)}) copy-start(bf16[640,1024]{1,0:T(8,128)(2,1)} %get-tuple-element.94) | copy-start | bytes 3932164
  268.7 12.8 %collective-permute-start.3 = (bf16[64,1024]{1,0:T(8,128)(2,1)}, bf16[64,1024]{1,0:T(8,128)(2,1)S(1)}, u32[]{:S(2)}, u32[]{:S(2)}) collective-permute-start(bf16[64,1024]{1,0:T(8,128)(2,1)} %broadcast_select_fusion), channel_id=1, source_target_pairs={{0,8},{4,12},{1,9},{5,13},{2,10},{6,14},{3,11},{7,15},{64,72},{68,... | collective-permute-start | bytes 393224 | tf_op jit(solution)/shard_map/ppermute | solution.py:30
  282.7 3.8 collective-permute-start.4
  286.5 4.2 collective-permute-start.5
  342.2 293.3 %reduce-scatter.2.cloned.1.call-start = ((), (), s32[]{:S(2)}) async-start(), calls=%async_computation.10 | async-start | bytes 6553600 | tf_op jit(solution)/shard_map/reduce_scatter | solution.py:165
  381.1 173.8 %all-to-all-start.6 = ((bf16[16,15,64,256]{3,2,1,0:T(8,128)(2,1)}), bf16[16,15,64,256]{3,2,1,0:T(8,128)(2,1)}, u32[]{:S(2)}, u32[]{:S(2)}) async-start(bf16[16,15,64,256]{3,2,1,0:T(8,128)(2,1)} %bitcast.268), calls=%async_computation.7 | async-start | bytes 15728640 | tf_op jit(solution)/shard_map/all_to_all | solution.py:281
  393.2 78.5 %collective-permute-start.6 = (f32[64,1024]{1,0:T(8,128)}, f32[64,1024]{1,0:T(8,128)S(1)}, u32[]{:S(2)}, u32[]{:S(2)}) collective-permute-start(f32[64,1024]{1,0:T(8,128)} %reshape.553), channel_id=1, source_target_pairs={{32,0},{36,4},{40,8},{44,12},{48,16},{52,20},{56,24},{60,28},{33,1... | collective-permute-start | bytes 786440 | tf_op jit(solution)/shard_map/ppermute | solution.py:43
  472.7 17.6 %copy-start.5 = (bf16[10,4,4,64,128]{4,3,2,1,0:T(8,128)(2,1)S(1)}, bf16[10,4,4,64,128]{4,3,2,1,0:T(8,128)(2,1)}, u32[]{:S(2)}) copy-start(bf16[10,4,4,64,128]{4,3,2,1,0:T(8,128)(2,1)} %copy-done.4) | copy-start | bytes 7864324
  472.7 17.6 %copy-start.13 = (bf16[4,10,64,4,64]{2,4,3,1,0:T(8,128)(2,1)S(1)}, bf16[4,10,64,4,64]{2,4,3,1,0:T(8,128)(2,1)}, u32[]{:S(2)}) copy-start(bf16[4,10,64,4,64]{2,4,3,1,0:T(8,128)(2,1)} %copy-done.12) | copy-start | bytes 3932164
  472.7 16.2 %collective-permute-start.7 = (f32[64,1024]{1,0:T(8,128)S(1)}, f32[64,1024]{1,0:T(8,128)S(1)}, u32[]{:S(2)}, u32[]{:S(2)}) collective-permute-start(f32[64,1024]{1,0:T(8,128)S(1)} %add.228), channel_id=1, source_target_pairs={{16,0},{20,4},{24,8},{28,12},{17,1},{21,5},{25,9},{29,13},{18,2},{... | collective-permute-start | bytes 786440 | tf_op jit(solution)/shard_map/ppermute | solution.py:43
  475.6 16.8 %copy-start.3 = (f32[12,64,2,4,128]{4,3,2,1,0:T(4,128)}, f32[12,64,2,4,128]{4,3,2,1,0:T(4,128)S(1)}, u32[]{:S(2)}) copy-start(f32[12,64,2,4,128]{4,3,2,1,0:T(4,128)S(1)} %fusion.11) | copy-start | bytes 9437188
  488.9 16.4 %collective-permute-start.8 = (f32[64,1024]{1,0:T(8,128)S(1)}, f32[64,1024]{1,0:T(8,128)S(1)}, u32[]{:S(2)}, u32[]{:S(2)}) collective-permute-start(f32[64,1024]{1,0:T(8,128)S(1)} %add.229), channel_id=1, source_target_pairs={{8,0},{12,4},{9,1},{13,5},{10,2},{14,6},{11,3},{15,7},{72,64},{76,... | collective-permute-start | bytes 786440 | tf_op jit(solution)/shard_map/ppermute | solution.py:43
  505.4 11.4 %collective-permute-start.9 = (f32[64,1024]{1,0:T(8,128)S(1)}, f32[64,1024]{1,0:T(8,128)S(1)}, u32[]{:S(2)}, u32[]{:S(2)}) collective-permute-start(f32[64,1024]{1,0:T(8,128)S(1)} %add.230), channel_id=1, source_target_pairs={{4,0},{5,1},{6,2},{7,3},{68,64},{69,65},{70,66},{71,67}} | collective-permute-start | bytes 786440 | tf_op jit(solution)/shard_map/ppermute | solution.py:43
  523.3 24.0 %collective-permute-start.11 = (bf16[64,1024]{1,0:T(8,128)(2,1)S(1)}, bf16[64,1024]{1,0:T(8,128)(2,1)}, u32[]{:S(2)}, u32[]{:S(2)}) collective-permute-start(bf16[64,1024]{1,0:T(8,128)(2,1)S(1)} %concatenate.41), channel_id=1, source_target_pairs={{4,0},{8,4},{12,8},{16,12},{20,16},{24,20},{28,24},{32,28},{36,32}... | collective-permute-start | bytes 393224 | tf_op jit(solution)/shard_map/ppermute | solution.py:19
  524.6 22.7 %collective-permute-start.10 = (bf16[64,1024]{1,0:T(8,128)(2,1)S(1)}, bf16[64,1024]{1,0:T(8,128)(2,1)}, u32[]{:S(2)}, u32[]{:S(2)}) collective-permute-start(bf16[64,1024]{1,0:T(8,128)(2,1)S(1)} %concatenate.40), channel_id=1, source_target_pairs={{0,4},{4,8},{8,12},{12,16},{16,20},{20,24},{24,28},{28,32},{32,36}... | collective-permute-start | bytes 393224 | tf_op jit(solution)/shard_map/ppermute | solution.py:16
  554.9 50.1 %all-to-all-start.5 = ((bf16[4,2,40960]{2,1,0:T(2,128)(2,1)}), bf16[4,2,40960]{2,1,0:T(2,128)(2,1)}, u32[]{:S(2)}, u32[]{:S(2)}) async-start(bf16[4,2,40960]{2,1,0:T(2,128)(2,1)} %reshape.599), calls=%async_computation.6 | async-start | bytes 1310720 | tf_op jit(solution)/shard_map/all_to_all | solution.py:290
  605.0 15.2 %all-to-all-start.8 = ((bf16[4,2,40960]{2,1,0:T(2,128)(2,1)}), bf16[4,2,40960]{2,1,0:T(2,128)(2,1)}, u32[]{:S(2)}, u32[]{:S(2)}) async-start(bf16[4,2,40960]{2,1,0:T(2,128)(2,1)} %reshape.603), calls=%async_computation.9 | async-start | bytes 1310720 | tf_op jit(solution)/shard_map/all_to_all | solution.py:292
  620.1 13.6 %all-to-all-start.7 = ((bf16[4,2,40960]{2,1,0:T(2,128)(2,1)}), bf16[4,2,40960]{2,1,0:T(2,128)(2,1)S(1)}, u32[]{:S(2)}, u32[]{:S(2)}) async-start(bf16[4,2,40960]{2,1,0:T(2,128)(2,1)} %reshape.601), calls=%async_computation.8 | async-start | bytes 1310720 | tf_op jit(solution)/shard_map/all_to_all | solution.py:291
  (25 other events, 114.6 us)
Sparse Core Ops, SparseCore 0:
  166.7 37.1 all-gather.1
  342.3 194.1 all-reduce.3
  538.9 61.0 reduce-scatter.1
where the time goes:
time: 657 us; the launch traced here: 645 us
  local copies, waits for them, and re-layouts  209 us (32%)
  waiting for transfers between devices  175 us (27%)
  other arithmetic  95.2 us (14%)
  starting transfers between devices  80.8 us (12%)
  matrix products  69.2 us (11%)
  between operations  15.3 us (2%)
    unnamed x92, local copies, waits for them, and re-layouts  111 us
    ppermute x4, waiting for transfers between devices, reduce_to_first(): block = block + lax.ppermute(block, axis, pairs)  95.5 us
    ppermute x4, waiting for transfers between devices, broadcast_first(): got = lax.ppermute(block, axis, pairs)  78.6 us
    unnamed x6, other arithmetic  51.8 us
    dot_general x1, local copies, waits for them, and re-layouts, per_device(): jnp.dot(serve_hot.T, incoming.reshape(slot_total, -1), preferred_element_...  13.9 us
  transfers between devices with their start and end apart: 24, of which 7 were waited for; matrix products, arithmetic and copies ran while one was open for 44% of the time, Pallas kernels for 0%

commit v1 on v0

--- a/solution.py
+++ b/solution.py
@@ -51,7 +51,12 @@
     seq_count = lax.axis_size("seq")
     seq_index = lax.axis_index("seq")
     q_heads, k_heads, v_heads = (
-        lax.all_to_all(queries, "head", split_axis=2, concat_axis=1, tiled=True),
+        jnp.concatenate(
+            lax.all_to_all(
+                jnp.stack(jnp.split(queries, lax.axis_size("head"), axis=2)), "head", 0, 0
+            ),
+            axis=1,
+        ),
         lax.all_to_all(key_rows, "head", split_axis=2, concat_axis=1, tiled=True),
         lax.all_to_all(values, "head", split_axis=2, concat_axis=1, tiled=True),
     )

time: 657 us -> 636 us (0.968)
  other arithmetic: 95.2 us -> 78.9 us
  waiting for transfers between devices: 175 us -> 187 us
  local copies, waits for them, and re-layouts: 209 us -> 200 us
    unnamed x92 -> x83, local copies, waits for them, and re-layouts: 111 us -> 94.5 us
    ppermute x4, waiting for transfers between devices: 78.6 us -> 94.2 us  [broadcast_first(): got = lax.ppermute(block, axis, pairs)]
    unnamed x6 -> x5, other arithmetic: 51.8 us -> 41.2 us
    all_to_all x3 -> x0, local copies, waits for them, and re-layouts: 10.5 us -> none  [per_device(): lax.all_to_all(queries, 'head', split_axis=2, concat_axis=1, tiled=True)]
    reshape x1, local copies, waits for them, and re-layouts: 1.81 us -> 10.4 us  [per_device(): grad_piece.reshape(block_count, block_len, head_count, head_dim)]
  transfers between devices with their start and end apart: 24 -> 24, of which waited for: 7 -> 7; matrix products, arithmetic and copies ran while one was open for 44% -> 43% of each run, Pallas kernels for 0% -> 0%
where the time goes in v1:
time: 636 us; the launch traced here: 625 us
  local copies, waits for them, and re-layouts  200 us (31%)
  waiting for transfers between devices  187 us (29%)
  starting transfers between devices  79.7 us (13%)
  other arithmetic  78.9 us (12%)
  matrix products  63.1 us (10%)
  between operations  15.3 us (2%)
    unnamed x83, local copies, waits for them, and re-layouts  94.5 us
    ppermute x4, waiting for transfers between devices, broadcast_first(): got = lax.ppermute(block, axis, pairs)  94.2 us
    ppermute x4, waiting for transfers between devices, reduce_to_first(): block = block + lax.ppermute(block, axis, pairs)  90.3 us
    unnamed x5, other arithmetic  41.2 us
    dot_general x1, local copies, waits for them, and re-layouts, per_device(): jnp.dot(serve_hot.T, incoming.reshape(slot_total, -1), preferred_element_...  14 us
  transfers between devices with their start and end apart: 24, of which 7 were waited for; matrix products, arithmetic and copies ran while one was open for 43% of the time, Pallas kernels for 0%

profile of v1, /device:TPU:0, one launch (start us, length us, event | category | flops | bytes accessed | tf_op | source)
XLA Modules:
  0.0 624.5 jit_solution(16771357670545297850)
XLA Ops:
  7.2 6.0 copy.153
  13.8 12.7 %reduce.18 = bf16[2048,160]{1,0:T(8,128)(2,1)S(1)} reduce(bf16[2048,1,160]{2,1,0:T(2,128)(2,1)} %bitcast.269, bf16[]{:T(256)} %broadcast.350), dimensions={1}, to_apply=%bitcast.224.reduce_sub_computation | reduce | bytes 1310722
  35.4 5.9 copy.156
  41.2 12.7 %reduce.19 = bf16[2048,160]{1,0:T(8,128)(2,1)S(1)} reduce(bf16[2048,1,160]{2,1,0:T(2,128)(2,1)} %bitcast.272, bf16[]{:T(256)} %broadcast.350), dimensions={1}, to_apply=%bitcast.222.reduce_sub_computation | reduce | bytes 1310722
  56.3 4.8 all-to-all-start.1
  72.3 7.9 %all-to-all-start.3 = ((s32[16,1,15]{2,1,0:T(1,128)}), s32[16,1,15]{2,1,0:T(1,128)S(1)}, u32[]{:S(2)}, u32[]{:S(2)}) async-start(s32[16,1,15]{2,1,0:T(1,128)} %bitcast.22), calls=%async_computation.3 | async-start | bytes 16384 | tf_op jit(solution)/shard_map/all_to_all | solution.py:87
  84.4 5.7 copy.157
  99.6 4.8 all-to-all-start.2
  119.9 5.3 convolution_convert_fusion.1
  125.3 8.7 %copy.260 = bf16[30,8,64,256]{3,2,1,0:T(8,128)(2,1)} copy(bf16[30,8,64,256]{3,1,2,0:T(8,128)(2,1)} %bitcast.249) | data formatting | bytes 15728640
  134.0 8.2 %all-to-all-start.4 = ((bf16[16,15,64,256]{3,2,1,0:T(8,128)(2,1)}), bf16[16,15,64,256]{3,2,1,0:T(8,128)(2,1)}, u32[]{:S(2)}, u32[]{:S(2)}) async-start(bf16[16,15,64,256]{3,2,1,0:T(8,128)(2,1)} %bitcast.252), calls=%async_computation.4 | async-start | bytes 15728640 | tf_op jit(solution)/shard_map/all_to_all | solution.py:102
  152.5 93.9 %collective-permute-done.2 = bf16[64,1024]{1,0:T(8,128)(2,1)S(1)} collective-permute-done((bf16[64,1024]{1,0:T(8,128)(2,1)S(1)}, bf16[64,1024]{1,0:T(8,128)(2,1)S(1)}, u32[]{:S(2)}, u32[]{:S(2)}) %collective-permute-start.2) | collective-permute-done | bytes 131104 | tf_op jit(solution)/shard_map/ppermute | solution.py:30
  255.3 4.9 pad_maximum_fusion.1
  276.1 10.4 %reshape.549 = bf16[10,64,4,128]{3,2,1,0:T(4,128)(2,1)S(1)} reshape(bf16[640,512]{1,0:T(8,128)(2,1)} %fusion.70) | data formatting | bytes 1310720 | tf_op jit(solution)/shard_map/reshape | solution.py:183
  286.5 14.4 %copy.261 = bf16[30,8,64,256]{3,1,2,0:T(8,128)(2,1)} copy(bf16[30,8,64,256]{3,2,1,0:T(8,128)(2,1)} %bitcast.110) | data formatting | bytes 15728640
  300.9 4.8 convolution_convert_fusion.2
  353.4 5.7 copy.265
  359.1 8.7 %all-to-all-start.6 = ((bf16[16,15,64,256]{3,2,1,0:T(8,128)(2,1)}), bf16[16,15,64,256]{3,2,1,0:T(8,128)(2,1)}, u32[]{:S(2)}, u32[]{:S(2)}) async-start(bf16[16,15,64,256]{3,2,1,0:T(8,128)(2,1)} %bitcast.251), calls=%async_computation.7 | async-start | bytes 15728640 | tf_op jit(solution)/shard_map/all_to_all | solution.py:286
  371.6 4.7 multiply_convert_fusion.2
  390.6 57.8 %collective-permute-done.6 = f32[64,1024]{1,0:T(8,128)S(1)} collective-permute-done((f32[64,1024]{1,0:T(8,128)}, f32[64,1024]{1,0:T(8,128)S(1)}, u32[]{:S(2)}, u32[]{:S(2)}) %collective-permute-start.6) | collective-permute-done | bytes 262176 | tf_op jit(solution)/shard_map/ppermute | solution.py:43
  452.0 14.3 %collective-permute-done.7 = f32[64,1024]{1,0:T(8,128)S(1)} collective-permute-done((f32[64,1024]{1,0:T(8,128)S(1)}, f32[64,1024]{1,0:T(8,128)S(1)}, u32[]{:S(2)}, u32[]{:S(2)}) %collective-permute-start.7) | collective-permute-done | bytes 262176 | tf_op jit(solution)/shard_map/ppermute | solution.py:43
  469.8 10.6 %collective-permute-done.8 = f32[64,1024]{1,0:T(8,128)S(1)} collective-permute-done((f32[64,1024]{1,0:T(8,128)S(1)}, f32[64,1024]{1,0:T(8,128)S(1)}, u32[]{:S(2)}, u32[]{:S(2)}) %collective-permute-start.8) | collective-permute-done | bytes 262176 | tf_op jit(solution)/shard_map/ppermute | solution.py:43
  483.6 7.7 %collective-permute-done.9 = f32[64,1024]{1,0:T(8,128)S(1)} collective-permute-done((f32[64,1024]{1,0:T(8,128)S(1)}, f32[64,1024]{1,0:T(8,128)S(1)}, u32[]{:S(2)}, u32[]{:S(2)}) %collective-permute-start.9) | collective-permute-done | bytes 262176 | tf_op jit(solution)/shard_map/ppermute | solution.py:43
  496.1 5.2 collective-permute-start.10
  506.4 4.9 broadcast_in_dim_reshape.6
  511.3 6.5 %reduce.20 = bf16[640,512]{1,0:T(8,128)(2,1)} reduce(bf16[640,1,512]{2,1,0:T(2,128)(2,1)} %bitcast.281, bf16[]{:T(256)} %broadcast.350), dimensions={1}, to_apply=%bitcast.226.reduce_sub_computation | reduce | bytes 1310722
  534.5 14.9 %copy.266 = bf16[30,8,64,256]{3,1,2,0:T(8,128)(2,1)} copy(bf16[30,8,64,256]{3,2,1,0:T(8,128)(2,1)} %bitcast.125) | data formatting | bytes 15728640
  549.5 14.0 %dot_general.103 = bf16[64,2,128,240]{2,1,0,3:T(2,128)(2,1)} reshape(bf16[16384,240]{0,1:T(8,128)(2,1)} %bitcast.253) | data formatting | bytes 15728640 | tf_op jit(solution)/shard_map/dot_general | solution.py:287
  563.5 9.4 %fusion.6 = bf16[10,64,2,4,128]{4,0,2,1,3:T(8,128)(2,1)S(1)} fusion(f32[10,64,2,4,128]{4,3,2,1,0:T(4,128)S(1)} %copy-done.19, bf16[64,2,128,240]{2,1,0,3:T(2,128)(2,1)} %dot_general.103, s32[10,4]{0,1:T(4,128)S(1)} %multiply_add_fusion, s32[240]{0:T(256)S(1)} %eq.85), kind=kOutput, calls=%fused_computation.16 | convolution fusion | flops 315893120 | bytes 11797600 | tf_op jit(solution)/shard_map/dot_general | solution.py:287
  580.1 5.4 all-to-all-start.8
  600.0 4.8 all-to-all-start.7
  604.8 5.0 broadcast_multiply_fusion
  (246 shorter events, 218.7 us)
Async XLA Ops:
  7.2 264.8 %copy-start = (bf16[512,2048]{1,0:T(8,128)(2,1)S(1)}, bf16[512,2048]{1,0:T(8,128)(2,1)}, u32[]{:S(2)}) copy-start(bf16[512,2048]{1,0:T(8,128)(2,1)} %param.22) | copy-start | bytes 6291460
  13.8 19.6 %copy-start.27 = (s32[10,4,4]{0,2,1:T(4,128)S(1)}, s32[10,4,4]{0,2,1:T(4,128)}, u32[]{:S(2)}) copy-start(s32[10,4,4]{0,2,1:T(4,128)} %param.21) | copy-start | bytes 1924
  28.8 27.4 %all-to-all-start = ((bf16[4,2,40960]{2,1,0:T(2,128)(2,1)}), bf16[4,2,40960]{2,1,0:T(2,128)(2,1)}, u32[]{:S(2)}, u32[]{:S(2)}) async-start(bf16[4,2,40960]{2,1,0:T(2,128)(2,1)} %reshape.595), calls=%async_computation | async-start | bytes 1310720 | tf_op jit(solution)/shard_map/all_to_all | solution.py:60
  56.3 16.0 %all-to-all-start.1 = ((bf16[4,2,40960]{2,1,0:T(2,128)(2,1)}), bf16[4,2,40960]{2,1,0:T(2,128)(2,1)}, u32[]{:S(2)}, u32[]{:S(2)}) async-start(bf16[4,2,40960]{2,1,0:T(2,128)(2,1)} %reshape.593), calls=%async_computation.1 | async-start | bytes 1310720 | tf_op jit(solution)/shard_map/all_to_all | solution.py:61
  72.3 20.1 %copy-start.15 = (bf16[1,4,160,512]{3,2,1,0:T(8,128)(2,1)}, bf16[1,4,160,512]{3,2,1,0:T(8,128)(2,1)S(1)}, u32[]{:S(2)}) copy-start(bf16[1,4,160,512]{3,2,1,0:T(8,128)(2,1)S(1)} %copy.155) | copy-start | bytes 1966084
  72.3 27.3 %all-to-all-start.3 = ((s32[16,1,15]{2,1,0:T(1,128)}), s32[16,1,15]{2,1,0:T(1,128)S(1)}, u32[]{:S(2)}, u32[]{:S(2)}) async-start(s32[16,1,15]{2,1,0:T(1,128)} %bitcast.22), calls=%async_computation.3 | async-start | bytes 16384 | tf_op jit(solution)/shard_map/all_to_all | solution.py:87
  93.2 12.5 %collective-permute-start = (bf16[64,1024]{1,0:T(8,128)(2,1)S(1)}, bf16[64,1024]{1,0:T(8,128)(2,1)S(1)}, u32[]{:S(2)}, u32[]{:S(2)}) collective-permute-start(bf16[64,1024]{1,0:T(8,128)(2,1)S(1)} %get-tuple-element.96), channel_id=1, source_target_pairs={{0,4},{4,8},{8,12},{12,16},{16,20},{20,24},{24,28},{28,32},{32,36}... | collective-permute-start | bytes 393224 | tf_op jit(solution)/shard_map/ppermute | solution.py:16
  97.3 9.0 %collective-permute-start.1 = (bf16[64,1024]{1,0:T(8,128)(2,1)S(1)}, bf16[64,1024]{1,0:T(8,128)(2,1)}, u32[]{:S(2)}, u32[]{:S(2)}) collective-permute-start(bf16[64,1024]{1,0:T(8,128)(2,1)S(1)} %get-tuple-element.97), channel_id=1, source_target_pairs={{4,0},{8,4},{12,8},{16,12},{20,16},{24,20},{28,24},{32,28},{36,32}... | collective-permute-start | bytes 393224 | tf_op jit(solution)/shard_map/ppermute | solution.py:19
  99.6 34.4 %all-to-all-start.2 = ((bf16[4,1,160,512]{3,2,1,0:T(8,128)(2,1)}), bf16[4,1,160,512]{3,2,1,0:T(8,128)(2,1)}, u32[]{:S(2)}, u32[]{:S(2)}) async-start(bf16[4,1,160,512]{3,2,1,0:T(8,128)(2,1)} %pad_maximum_fusion.7), calls=%async_computation.2 | async-start | bytes 1310720 | tf_op jit(solution)/shard_map/all_to_all | solution.py:55
  134.0 13.1 %copy-start.29 = (s32[160]{0:T(256)S(1)}, s32[160]{0:T(256)}, u32[]{:S(2)}) copy-start(s32[160]{0:T(256)} %copy-done.28) | copy-start | bytes 1924
  134.0 152.5 %all-to-all-start.4 = ((bf16[16,15,64,256]{3,2,1,0:T(8,128)(2,1)}), bf16[16,15,64,256]{3,2,1,0:T(8,128)(2,1)}, u32[]{:S(2)}, u32[]{:S(2)}) async-start(bf16[16,15,64,256]{3,2,1,0:T(8,128)(2,1)} %bitcast.252), calls=%async_computation.4 | async-start | bytes 15728640 | tf_op jit(solution)/shard_map/all_to_all | solution.py:102
  142.2 129.8 %all-gather.2.cloned.1.call-start = ((), (), s32[]{:S(2)}) async-start(), calls=%async_computation.11 | async-start | bytes 3276800 | tf_op jit(solution)/shard_map/all_gather | solution.py:176
  142.9 461.9 %all-reduce.4.cloned.1.call-start = ((), (), s32[]{:S(2)}) async-start(), calls=%async_computation.12 | async-start | bytes 8388608 | tf_op jit(solution)/shard_map/psum | solution.py:182
  143.3 103.2 %collective-permute-start.2 = (bf16[64,1024]{1,0:T(8,128)(2,1)S(1)}, bf16[64,1024]{1,0:T(8,128)(2,1)S(1)}, u32[]{:S(2)}, u32[]{:S(2)}) collective-permute-start(bf16[64,1024]{1,0:T(8,128)(2,1)S(1)} %get-tuple-element.97), channel_id=1, source_target_pairs={{0,4},{1,5},{2,6},{3,7},{64,68},{65,69},{66,70},{67,71}} | collective-permute-start | bytes 393224 | tf_op jit(solution)/shard_map/ppermute | solution.py:30
  246.5 14.8 %collective-permute-start.3 = (bf16[64,1024]{1,0:T(8,128)(2,1)S(1)}, bf16[64,1024]{1,0:T(8,128)(2,1)S(1)}, u32[]{:S(2)}, u32[]{:S(2)}) collective-permute-start(bf16[64,1024]{1,0:T(8,128)(2,1)S(1)} %broadcast_select_fusion), channel_id=1, source_target_pairs={{0,8},{4,12},{1,9},{5,13},{2,10},{6,14},{3,11},{7,15},{64,72},{68,... | collective-permute-start | bytes 393224 | tf_op jit(solution)/shard_map/ppermute | solution.py:30
  261.3 3.8 collective-permute-start.4
  265.1 4.2 collective-permute-start.5
  330.5 284.8 %reduce-scatter.2.cloned.1.call-start = ((), (), s32[]{:S(2)}) async-start(), calls=%async_computation.10 | async-start | bytes 6553600 | tf_op jit(solution)/shard_map/reduce_scatter | solution.py:170
  359.1 171.0 %all-to-all-start.6 = ((bf16[16,15,64,256]{3,2,1,0:T(8,128)(2,1)}), bf16[16,15,64,256]{3,2,1,0:T(8,128)(2,1)}, u32[]{:S(2)}, u32[]{:S(2)}) async-start(bf16[16,15,64,256]{3,2,1,0:T(8,128)(2,1)} %bitcast.251), calls=%async_computation.7 | async-start | bytes 15728640 | tf_op jit(solution)/shard_map/all_to_all | solution.py:286
  370.3 78.0 %collective-permute-start.6 = (f32[64,1024]{1,0:T(8,128)}, f32[64,1024]{1,0:T(8,128)S(1)}, u32[]{:S(2)}, u32[]{:S(2)}) collective-permute-start(f32[64,1024]{1,0:T(8,128)} %reshape.552), channel_id=1, source_target_pairs={{32,0},{36,4},{40,8},{44,12},{48,16},{52,20},{56,24},{60,28},{33,1... | collective-permute-start | bytes 786440 | tf_op jit(solution)/shard_map/ppermute | solution.py:43
  449.3 18.4 %copy-start.3 = (bf16[10,4,4,64,128]{4,3,2,1,0:T(8,128)(2,1)S(1)}, bf16[10,4,4,64,128]{4,3,2,1,0:T(8,128)(2,1)}, u32[]{:S(2)}) copy-start(bf16[10,4,4,64,128]{4,3,2,1,0:T(8,128)(2,1)} %copy-done.2) | copy-start | bytes 7864324
  449.3 18.4 %copy-start.5 = (bf16[4,10,64,4,64]{2,4,3,1,0:T(8,128)(2,1)S(1)}, bf16[4,10,64,4,64]{2,4,3,1,0:T(8,128)(2,1)}, u32[]{:S(2)}) copy-start(bf16[4,10,64,4,64]{2,4,3,1,0:T(8,128)(2,1)} %copy-done.4) | copy-start | bytes 3932164
  449.3 16.9 %collective-permute-start.7 = (f32[64,1024]{1,0:T(8,128)S(1)}, f32[64,1024]{1,0:T(8,128)S(1)}, u32[]{:S(2)}, u32[]{:S(2)}) collective-permute-start(f32[64,1024]{1,0:T(8,128)S(1)} %add.228), channel_id=1, source_target_pairs={{16,0},{20,4},{24,8},{28,12},{17,1},{21,5},{25,9},{29,13},{18,2},{... | collective-permute-start | bytes 786440 | tf_op jit(solution)/shard_map/ppermute | solution.py:43
  466.3 15.9 %copy-start.21 = (bf16[4,10,64,64]{2,3,1,0:T(8,128)(2,1)S(1)}, bf16[4,10,64,64]{2,3,1,0:T(8,128)(2,1)}, u32[]{:S(2)}) copy-start(bf16[4,10,64,64]{2,3,1,0:T(8,128)(2,1)} %copy-done.20) | copy-start | bytes 983044
  466.3 14.1 %collective-permute-start.8 = (f32[64,1024]{1,0:T(8,128)S(1)}, f32[64,1024]{1,0:T(8,128)S(1)}, u32[]{:S(2)}, u32[]{:S(2)}) collective-permute-start(f32[64,1024]{1,0:T(8,128)S(1)} %add.229), channel_id=1, source_target_pairs={{8,0},{12,4},{9,1},{13,5},{10,2},{14,6},{11,3},{15,7},{72,64},{76,... | collective-permute-start | bytes 786440 | tf_op jit(solution)/shard_map/ppermute | solution.py:43
  480.4 10.8 %collective-permute-start.9 = (f32[64,1024]{1,0:T(8,128)S(1)}, f32[64,1024]{1,0:T(8,128)S(1)}, u32[]{:S(2)}, u32[]{:S(2)}) collective-permute-start(f32[64,1024]{1,0:T(8,128)S(1)} %add.230), channel_id=1, source_target_pairs={{4,0},{5,1},{6,2},{7,3},{68,64},{69,65},{70,66},{71,67}} | collective-permute-start | bytes 786440 | tf_op jit(solution)/shard_map/ppermute | solution.py:43
  494.8 31.9 %collective-permute-start.11 = (bf16[64,1024]{1,0:T(8,128)(2,1)S(1)}, bf16[64,1024]{1,0:T(8,128)(2,1)S(1)}, u32[]{:S(2)}, u32[]{:S(2)}) collective-permute-start(bf16[64,1024]{1,0:T(8,128)(2,1)S(1)} %concatenate.41), channel_id=1, source_target_pairs={{4,0},{8,4},{12,8},{16,12},{20,16},{24,20},{28,24},{32,28},{36,32}... | collective-permute-start | bytes 393224 | tf_op jit(solution)/shard_map/ppermute | solution.py:19
  496.1 30.6 %collective-permute-start.10 = (bf16[64,1024]{1,0:T(8,128)(2,1)S(1)}, bf16[64,1024]{1,0:T(8,128)(2,1)}, u32[]{:S(2)}, u32[]{:S(2)}) collective-permute-start(bf16[64,1024]{1,0:T(8,128)(2,1)S(1)} %concatenate.40), channel_id=1, source_target_pairs={{0,4},{4,8},{8,12},{12,16},{16,20},{20,24},{24,28},{28,32},{32,36}... | collective-permute-start | bytes 393224 | tf_op jit(solution)/shard_map/ppermute | solution.py:16
  530.1 50.0 %all-to-all-start.5 = ((bf16[4,2,40960]{2,1,0:T(2,128)(2,1)}), bf16[4,2,40960]{2,1,0:T(2,128)(2,1)}, u32[]{:S(2)}, u32[]{:S(2)}) async-start(bf16[4,2,40960]{2,1,0:T(2,128)(2,1)} %reshape.597), calls=%async_computation.6 | async-start | bytes 1310720 | tf_op jit(solution)/shard_map/all_to_all | solution.py:295
  549.5 14.0 %copy-start.19 = (f32[10,64,2,4,128]{4,3,2,1,0:T(4,128)S(1)}, f32[10,64,2,4,128]{4,3,2,1,0:T(4,128)}, u32[]{:S(2)}) copy-start(f32[10,64,2,4,128]{4,3,2,1,0:T(4,128)} %reshape.555) | copy-start | bytes 7864324
  580.1 19.9 %all-to-all-start.8 = ((bf16[4,2,40960]{2,1,0:T(2,128)(2,1)}), bf16[4,2,40960]{2,1,0:T(2,128)(2,1)S(1)}, u32[]{:S(2)}, u32[]{:S(2)}) async-start(bf16[4,2,40960]{2,1,0:T(2,128)(2,1)} %reshape.601), calls=%async_computation.9 | async-start | bytes 1310720 | tf_op jit(solution)/shard_map/all_to_all | solution.py:297
  600.0 13.6 %all-to-all-start.7 = ((bf16[4,2,40960]{2,1,0:T(2,128)(2,1)}), bf16[4,2,40960]{2,1,0:T(2,128)(2,1)S(1)}, u32[]{:S(2)}, u32[]{:S(2)}) async-start(bf16[4,2,40960]{2,1,0:T(2,128)(2,1)} %reshape.599), calls=%async_computation.8 | async-start | bytes 1310720 | tf_op jit(solution)/shard_map/all_to_all | solution.py:296
  (22 other events, 71.1 us)
Sparse Core Ops, SparseCore 0:
  144.6 37.1 all-gather.1
  330.7 195.9 all-reduce.3
  529.0 58.2 reduce-scatter.1
